TPU v7x, 512 devices: a whole 4x4x16 slice. The times are simulated.
512 devices in a mesh: outer: 16 (over z), inner: 32 (over y, x, core).
Axes of the slice: x: 4, y: 4, z: 16, core: 2. Of those that a mesh axis runs over, the one named last changes fastest.
Arguments:
- field_slab: float32 [512, 128, 4096], P(None, 'inner', 'outer'), may hold values from -48 to 48, as said below
- start_block: float32 [512, 256], replicated, may hold values from -6 to 6
Outputs:
- factor: float32 [512, 256], replicated
- core_fibres: float32 [256, 128, 4096], P('inner', None, 'outer')
Inputs may be any that keep to these rules, and one draw needn't show every extreme that they name: `field_slab`: real values.
All inputs are finite; a program needn't handle non-finite values.
Results may differ from a plain program's by a relative error of at most 0.00016.
Values sent between devices are 32-bit elements; how exact they have to be, the bound alone decides.
No kernel may reach another device: no remote copies, remote signals or barrier semaphores. Data moves between devices by JAX's collectives and lax.ppermute only.
A program may use at most 64 MiB of HBM per device.

v0:
```python
import jax
import jax.numpy as jnp
from jax import lax
from jax.sharding import PartitionSpec as P

ITERS = 2


def product(first_mat, second_mat):
    return jnp.dot(
        first_mat, second_mat, precision=lax.Precision.HIGHEST, preferred_element_type=jnp.float32
    )


def orthonormal(block):
    chol_factor = jnp.linalg.cholesky(product(block.T, block))
    return lax.linalg.triangular_solve(
        chol_factor, block, left_side=False, lower=True, transpose_a=True
    )


def on_device(field_slab, start_block):
    order_rows = field_slab.shape[0]
    local_shape = field_slab.shape
    unfolded = field_slab.reshape(order_rows, local_shape[1] * local_shape[2])
    gram_local = product(unfolded, unfolded.T)
    subspace = orthonormal(start_block)
    gram_total = lax.psum(gram_local, ("outer", "inner"))
    for sweep_index in range(ITERS):
        subspace = orthonormal(product(gram_total, subspace))
    core_block = product(subspace.T, unfolded).reshape(
        subspace.shape[1], local_shape[1], local_shape[2]
    )
    core_fibres = lax.all_to_all(core_block, "inner", split_axis=0, concat_axis=1, tiled=True)
    return (subspace, core_fibres)


def solution(mesh):
    in_specs = (P(None, "inner", "outer"), P())
    out_specs = (P(), P("inner", None, "outer"))
    return jax.shard_map(
        on_device, mesh=mesh, in_specs=in_specs, out_specs=out_specs, check_vma=False
    )
```

profile of v0, /device:TPU:1, one launch (start us, length us, event | category | flops | bytes accessed | tf_op | source)
XLA Modules:
  0.0 663.9 jit_solution(16527323154972641272)
XLA Ops:
  7.2 7.2 %fusion.2 = f32[512,512]{1,0:T(8,128)} fusion(f32[512,4,256]{2,1,0:T(4,128)} %param.5), kind=kOutput, calls=%fused_computation.8 | convolution fusion | flops 3221225472 | bytes 3145728 | tf_op jit(solution)/shard_map/dot_general | solution.py:10
  14.4 1.0 fusion.52
  15.4 0.1 copy.14
  15.7 11.7 %cholesky.172 = f32[128,128]{1,0:T(8,128)S(1)} custom-call(f32[128,128]{1,0:T(8,128)S(1)} %cholesky.270), custom_call_target="Cholesky" | custom-call | tf_op jit(solution)/shard_map/jit(cholesky)/cholesky | solution.py:16
  27.4 9.8 %custom-call.15 = f32[1,128,128]{1,2,0:T(8,128)S(1)} custom-call(f32[1,128,128]{2,1,0:T(8,128)S(1)} %get-tuple-element.72), custom_call_target="InvertDiagBlocksLowerTriangular" | custom-call | tf_op jit(solution)/shard_map/jit(cholesky)/cholesky | solution.py:16
  37.2 0.2 constant_dynamic-update-slice_fusion.5
  37.5 0.3 convolution_subtract_fusion.5
  37.7 12.0 %cholesky.189 = f32[128,128]{1,0:T(8,128)S(1)} custom-call(f32[128,128]{1,0:T(8,128)S(1)} %convolution_subtract_fusion.5), custom_call_target="Cholesky" | custom-call | tf_op jit(solution)/shard_map/jit(cholesky)/cholesky | solution.py:16
  49.7 0.7 compare_reduce_fusion.4
  51.7 3.8 while.6
  51.7 0.6 fusion.79
  52.3 1.3 bitcast_dynamic-update-slice_fusion.6
  53.6 0.6 fusion.79
  54.2 1.3 bitcast_dynamic-update-slice_fusion.6
  55.5 19.7 %custom-call.16 = f32[2,128,128]{1,2,0:T(8,128)S(1)} custom-call(f32[2,128,128]{2,1,0:T(8,128)S(1)} %get-tuple-element.24), custom_call_target="InvertDiagBlocksLowerTriangular" | custom-call | tf_op jit(solution)/shard_map/triangular_solve/custom-call.0 | solution.py:17
  75.2 0.4 fusion.22
  75.6 1.8 copy.21
  77.4 1.9 copy.17
  79.4 0.6 convolution_subtract_fusion.2
  80.0 0.4 fusion.32
  80.4 406.9 %all-reduce.3.cloned.1.call-done = f32[512,512]{1,0:T(8,128)} async-done(((f32[512,512]{1,0:T(8,128)}), f32[512,512]{1,0:T(8,128)}) %all-reduce.3.cloned.1.call-update) | async-done | bytes 1048592 | tf_op jit(solution)/shard_map/psum | solution.py:28
  487.3 2.2 fusion.5
  489.5 1.0 fusion.53
  490.8 11.7 %cholesky.206 = f32[128,128]{1,0:T(8,128)S(1)} custom-call(f32[128,128]{1,0:T(8,128)S(1)} %cholesky.273), custom_call_target="Cholesky" | custom-call | tf_op jit(solution)/shard_map/jit(cholesky)/cholesky | solution.py:16
  502.5 9.8 %custom-call.17 = f32[1,128,128]{1,2,0:T(8,128)S(1)} custom-call(f32[1,128,128]{2,1,0:T(8,128)S(1)} %get-tuple-element.68), custom_call_target="InvertDiagBlocksLowerTriangular" | custom-call | tf_op jit(solution)/shard_map/jit(cholesky)/cholesky | solution.py:16
  512.3 0.2 constant_dynamic-update-slice_fusion.3
  512.6 0.3 convolution_subtract_fusion.4
  512.8 22.6 %cholesky.223 = f32[128,128]{1,0:T(8,128)S(1)} custom-call(f32[128,128]{1,0:T(8,128)S(1)} %convolution_subtract_fusion.4), custom_call_target="Cholesky" | custom-call | tf_op jit(solution)/shard_map/jit(cholesky)/cholesky | solution.py:16
  535.5 0.7 compare_reduce_fusion.2
  536.2 0.6 compare_reduce_fusion.3
  538.2 4.1 while.7
  538.3 0.6 fusion.80
  538.9 1.4 bitcast_dynamic-update-slice_fusion.7
  540.3 0.6 fusion.80
  540.9 1.4 bitcast_dynamic-update-slice_fusion.7
  542.4 19.7 %custom-call.18 = f32[2,128,128]{1,2,0:T(8,128)S(1)} custom-call(f32[2,128,128]{2,1,0:T(8,128)S(1)} %get-tuple-element.25), custom_call_target="InvertDiagBlocksLowerTriangular" | custom-call | tf_op jit(solution)/shard_map/triangular_solve/custom-call.0 | solution.py:17
  562.1 0.4 fusion.17
  562.5 0.6 convolution_subtract_fusion.1
  563.1 0.4 fusion.28
  563.5 1.0 fusion.9
  564.5 1.0 fusion.54
  565.8 11.7 %cholesky.240 = f32[128,128]{1,0:T(8,128)S(1)} custom-call(f32[128,128]{1,0:T(8,128)S(1)} %cholesky.276), custom_call_target="Cholesky" | custom-call | tf_op jit(solution)/shard_map/jit(cholesky)/cholesky | solution.py:16
  577.5 9.8 %custom-call.19 = f32[1,128,128]{1,2,0:T(8,128)S(1)} custom-call(f32[1,128,128]{2,1,0:T(8,128)S(1)} %get-tuple-element.64), custom_call_target="InvertDiagBlocksLowerTriangular" | custom-call | tf_op jit(solution)/shard_map/jit(cholesky)/cholesky | solution.py:16
  587.3 0.2 constant_dynamic-update-slice_fusion
  587.6 0.3 convolution_subtract_fusion.3
  587.8 11.9 %cholesky.257 = f32[128,128]{1,0:T(8,128)S(1)} custom-call(f32[128,128]{1,0:T(8,128)S(1)} %convolution_subtract_fusion.3), custom_call_target="Cholesky" | custom-call | tf_op jit(solution)/shard_map/jit(cholesky)/cholesky | solution.py:16
  599.8 0.7 compare_reduce_fusion
  600.5 0.6 compare_reduce_fusion.1
  602.5 4.1 while.8
  602.5 0.6 fusion.81
  603.1 1.4 bitcast_dynamic-update-slice_fusion.8
  604.6 0.6 fusion.81
  605.2 1.4 bitcast_dynamic-update-slice_fusion.8
  606.6 19.7 %custom-call.20 = f32[2,128,128]{1,2,0:T(8,128)S(1)} custom-call(f32[2,128,128]{2,1,0:T(8,128)S(1)} %get-tuple-element.26), custom_call_target="InvertDiagBlocksLowerTriangular" | custom-call | tf_op jit(solution)/shard_map/triangular_solve/custom-call.0 | solution.py:17
  626.3 0.4 fusion.15
  626.7 0.6 convolution_subtract_fusion
  627.3 0.4 fusion.24
  627.8 1.9 fusion.13
  629.7 1.6 copy.18
  631.3 6.6 %all-to-all-start = ((f32[256,4,256]{2,1,0:T(4,128)}), f32[256,4,256]{2,1,0:T(4,128)S(1)}, u32[]{:S(2)}, u32[]{:S(2)}) async-start(f32[256,4,256]{2,1,0:T(4,128)} %copy.18), calls=%async_computation | async-start | bytes 2097152 | tf_op jit(solution)/shard_map/all_to_all | solution.py:34
  638.0 1.0 copy.20
  639.0 16.1 %all-to-all-done = f32[256,4,256]{2,1,0:T(4,128)S(1)} async-done(((f32[256,4,256]{2,1,0:T(4,128)}), f32[256,4,256]{2,1,0:T(4,128)S(1)}, u32[]{:S(2)}, u32[]{:S(2)}) %all-to-all-start) | async-done | bytes 1048608 | tf_op jit(solution)/shard_map/all_to_all | solution.py:34
  655.2 0.2 copy.19
  655.4 1.3 all_to_all.16
  (40 shorter events, 1.0 us)
Async XLA Ops:
  7.2 7.2 %copy-start = (f32[512,256]{1,0:T(8,128)S(1)}, f32[512,256]{1,0:T(8,128)}, u32[]{:S(2)}) copy-start(f32[512,256]{1,0:T(8,128)} %param.6) | copy-start | bytes 1572868
  7.2 480.1 %all-reduce.3.cloned.1.call-start = ((), (), s32[]{:S(2)}) async-start(), calls=%async_computation.1 | async-start | bytes 2097152 | tf_op jit(solution)/shard_map/psum | solution.py:28
  15.6 60.0 %copy-start.2 = (f32[512,4,256]{2,1,0:T(4,128)S(1)}, f32[512,4,256]{2,1,0:T(4,128)}, u32[]{:S(2)}) copy-start(f32[512,4,256]{2,1,0:T(4,128)} %param.5) | copy-start | bytes 6291460
  562.0 1.4 copy-start.1
  631.3 23.8 %all-to-all-start = ((f32[256,4,256]{2,1,0:T(4,128)}), f32[256,4,256]{2,1,0:T(4,128)S(1)}, u32[]{:S(2)}, u32[]{:S(2)}) async-start(f32[256,4,256]{2,1,0:T(4,128)} %copy.18), calls=%async_computation | async-start | bytes 2097152 | tf_op jit(solution)/shard_map/all_to_all | solution.py:34
Sparse Core Ops, SparseCore 0:
  14.5 472.7 all-reduce.2
where the time goes:
time: 673 us; the launch traced here: 664 us
  waiting for transfers between devices  423 us (63%)
  other arithmetic  174 us (26%)
  matrix products  21.1 us (3%)
  local copies, waits for them, and re-layouts  20.3 us (3%)
  between operations  18.7 us (3%)
    psum x1, waiting for transfers between devices, on_device(): gram_total = lax.psum(gram_local, ('outer', 'inner'))  407 us
    another operation x20, other arithmetic, orthonormal(): chol_factor = jnp.linalg.cholesky(product(block.T, block))  115 us
    another operation x8, other arithmetic, orthonormal(): lax.linalg.triangular_solve(chol_factor, block, left_side=False, lower=Tr...  59.2 us
    all_to_all x1, waiting for transfers between devices, on_device(): lax.all_to_all(core_block, 'inner', split_axis=0, concat_axis=1, tiled=True)  16.1 us
    dot_general x7, matrix products, product(): jnp.dot(first_mat, second_mat, precision=lax.Precision.HIGHEST, preferred...  15.4 us
  transfers between devices with their start and end apart: 2, of which 2 were waited for; matrix products, arithmetic and copies ran while one was open for 10% of the time, Pallas kernels for 0%

commit v1 on v0

--- a/solution.py
+++ b/solution.py
@@ -25,7 +25,7 @@
     unfolded = field_slab.reshape(order_rows, local_shape[1] * local_shape[2])
     gram_local = product(unfolded, unfolded.T)
     subspace = orthonormal(start_block)
-    gram_total = lax.psum(gram_local, ("outer", "inner"))
+    gram_total = lax.psum(lax.psum(gram_local, "inner"), "outer")
     for sweep_index in range(ITERS):
         subspace = orthonormal(product(gram_total, subspace))
     core_block = product(subspace.T, unfolded).reshape(

time: 673 us -> 467 us (0.69)
  waiting for transfers between devices: 423 us -> 223 us
  other arithmetic: 174 us -> 163 us
  starting transfers between devices: 6.68 us -> 17.4 us
    psum x1 -> x2, waiting for transfers between devices: 407 us -> 206 us  [on_device(): gram_total = lax.psum(lax.psum(gram_local, 'inner'), 'outer')]
    another operation x20, other arithmetic: 115 us -> 104 us  [orthonormal(): chol_factor = jnp.linalg.cholesky(product(block.T, block))]
    all_to_all x1, starting transfers between devices: 6.64 us -> 17.2 us  [on_device(): lax.all_to_all(core_block, 'inner', split_axis=0, concat_axis=1, tiled=True)]
  transfers between devices with their start and end apart: 2 -> 3, of which waited for: 2 -> 3; matrix products, arithmetic and copies ran while one was open for 10% -> 14% of each run, Pallas kernels for 0% -> 0%
where the time goes in v1:
time: 467 us; the launch traced here: 463 us
  waiting for transfers between devices  223 us (48%)
  other arithmetic  163 us (35%)
  matrix products  21.1 us (5%)
  local copies, waits for them, and re-layouts  20.3 us (4%)
  between operations  18.5 us (4%)
  starting transfers between devices  17.4 us (4%)
    psum x2, waiting for transfers between devices, on_device(): gram_total = lax.psum(lax.psum(gram_local, 'inner'), 'outer')  206 us
    another operation x20, other arithmetic, orthonormal(): chol_factor = jnp.linalg.cholesky(product(block.T, block))  104 us
    another operation x8, other arithmetic, orthonormal(): lax.linalg.triangular_solve(chol_factor, block, left_side=False, lower=Tr...  59.2 us
    all_to_all x1, starting transfers between devices, on_device(): lax.all_to_all(core_block, 'inner', split_axis=0, concat_axis=1, tiled=True)  17.2 us
    all_to_all x1, waiting for transfers between devices, on_device(): lax.all_to_all(core_block, 'inner', split_axis=0, concat_axis=1, tiled=True)  16.1 us
    dot_general x7, matrix products, product(): jnp.dot(first_mat, second_mat, precision=lax.Precision.HIGHEST, preferred...  15.4 us
    another operation x22, local copies, waits for them, and re-layouts, orthonormal(): lax.linalg.triangular_solve(chol_factor, block, left_side=False, lower=Tr...  12 us
  transfers between devices with their start and end apart: 3, of which 3 were waited for; matrix products, arithmetic and copies ran while one was open for 14% of the time, Pallas kernels for 0%

profile of v1, /device:TPU:1, one launch (start us, length us, event | category | flops | bytes accessed | tf_op | source)
XLA Modules:
  0.0 463.4 jit_solution(2082989754253744976)
XLA Ops:
  7.2 7.2 %fusion.2 = f32[512,512]{1,0:T(8,128)} fusion(f32[512,4,256]{2,1,0:T(4,128)} %param.5), kind=kOutput, calls=%fused_computation.8 | convolution fusion | flops 3221225472 | bytes 3145728 | tf_op jit(solution)/shard_map/dot_general | solution.py:10
  14.4 0.2 all-reduce.6.cloned.1.call-start
  14.6 1.0 fusion.52
  15.9 11.7 %cholesky.172 = f32[128,128]{1,0:T(8,128)S(1)} custom-call(f32[128,128]{1,0:T(8,128)S(1)} %cholesky.270), custom_call_target="Cholesky" | custom-call | tf_op jit(solution)/shard_map/jit(cholesky)/cholesky | solution.py:16
  27.6 9.8 %custom-call.15 = f32[1,128,128]{1,2,0:T(8,128)S(1)} custom-call(f32[1,128,128]{2,1,0:T(8,128)S(1)} %get-tuple-element.72), custom_call_target="InvertDiagBlocksLowerTriangular" | custom-call | tf_op jit(solution)/shard_map/jit(cholesky)/cholesky | solution.py:16
  37.5 0.2 constant_dynamic-update-slice_fusion.5
  37.7 0.3 convolution_subtract_fusion.5
  37.9 11.7 %cholesky.189 = f32[128,128]{1,0:T(8,128)S(1)} custom-call(f32[128,128]{1,0:T(8,128)S(1)} %convolution_subtract_fusion.5), custom_call_target="Cholesky" | custom-call | tf_op jit(solution)/shard_map/jit(cholesky)/cholesky | solution.py:16
  49.7 0.7 compare_reduce_fusion.4
  51.6 104.0 %all-reduce.4.cloned.1.call-done = f32[512,512]{1,0:T(8,128)} async-done(((f32[512,512]{1,0:T(8,128)}), f32[512,512]{1,0:T(8,128)}) %all-reduce.4.cloned.1.call-update) | async-done | bytes 1048592 | tf_op jit(solution)/shard_map/psum | solution.py:28
  155.7 4.2 while.6
  156.2 0.6 fusion.79
  156.7 1.3 bitcast_dynamic-update-slice_fusion.6
  158.1 0.6 fusion.79
  158.7 1.3 bitcast_dynamic-update-slice_fusion.6
  160.0 19.7 %custom-call.16 = f32[2,128,128]{1,2,0:T(8,128)S(1)} custom-call(f32[2,128,128]{2,1,0:T(8,128)S(1)} %get-tuple-element.24), custom_call_target="InvertDiagBlocksLowerTriangular" | custom-call | tf_op jit(solution)/shard_map/triangular_solve/custom-call.0 | solution.py:17
  179.7 1.8 copy.21
  181.5 1.9 copy.17
  183.4 0.4 fusion.22
  183.8 0.6 convolution_subtract_fusion.2
  184.4 0.4 fusion.32
  184.9 102.4 %all-reduce.6.cloned.1.call-done = f32[512,512]{1,0:T(8,128)} async-done(((f32[512,512]{1,0:T(8,128)}), f32[512,512]{1,0:T(8,128)}) %all-reduce.6.cloned.1.call-update) | async-done | bytes 1048592 | tf_op jit(solution)/shard_map/psum | solution.py:28
  287.2 2.2 fusion.5
  289.5 1.0 fusion.53
  290.7 11.7 %cholesky.206 = f32[128,128]{1,0:T(8,128)S(1)} custom-call(f32[128,128]{1,0:T(8,128)S(1)} %cholesky.273), custom_call_target="Cholesky" | custom-call | tf_op jit(solution)/shard_map/jit(cholesky)/cholesky | solution.py:16
  302.5 9.8 %custom-call.17 = f32[1,128,128]{1,2,0:T(8,128)S(1)} custom-call(f32[1,128,128]{2,1,0:T(8,128)S(1)} %get-tuple-element.68), custom_call_target="InvertDiagBlocksLowerTriangular" | custom-call | tf_op jit(solution)/shard_map/jit(cholesky)/cholesky | solution.py:16
  312.3 0.2 constant_dynamic-update-slice_fusion.3
  312.5 0.3 convolution_subtract_fusion.4
  312.8 11.9 %cholesky.223 = f32[128,128]{1,0:T(8,128)S(1)} custom-call(f32[128,128]{1,0:T(8,128)S(1)} %convolution_subtract_fusion.4), custom_call_target="Cholesky" | custom-call | tf_op jit(solution)/shard_map/jit(cholesky)/cholesky | solution.py:16
  324.7 0.6 compare_reduce_fusion.2
  325.3 0.7 compare_reduce_fusion.3
  327.4 4.1 while.7
  327.4 0.7 fusion.80
  328.0 1.3 bitcast_dynamic-update-slice_fusion.7
  329.4 0.7 fusion.80
  330.1 1.3 bitcast_dynamic-update-slice_fusion.7
  331.4 19.7 %custom-call.18 = f32[2,128,128]{1,2,0:T(8,128)S(1)} custom-call(f32[2,128,128]{2,1,0:T(8,128)S(1)} %get-tuple-element.25), custom_call_target="InvertDiagBlocksLowerTriangular" | custom-call | tf_op jit(solution)/shard_map/triangular_solve/custom-call.0 | solution.py:17
  351.1 0.4 fusion.17
  351.6 0.6 convolution_subtract_fusion.1
  352.1 0.4 fusion.28
  352.6 1.0 fusion.9
  353.6 1.0 fusion.54
  354.8 11.7 %cholesky.240 = f32[128,128]{1,0:T(8,128)S(1)} custom-call(f32[128,128]{1,0:T(8,128)S(1)} %cholesky.276), custom_call_target="Cholesky" | custom-call | tf_op jit(solution)/shard_map/jit(cholesky)/cholesky | solution.py:16
  366.6 9.8 %custom-call.19 = f32[1,128,128]{1,2,0:T(8,128)S(1)} custom-call(f32[1,128,128]{2,1,0:T(8,128)S(1)} %get-tuple-element.64), custom_call_target="InvertDiagBlocksLowerTriangular" | custom-call | tf_op jit(solution)/shard_map/jit(cholesky)/cholesky | solution.py:16
  376.4 0.2 constant_dynamic-update-slice_fusion
  376.6 0.3 convolution_subtract_fusion.3
  376.9 11.9 %cholesky.257 = f32[128,128]{1,0:T(8,128)S(1)} custom-call(f32[128,128]{1,0:T(8,128)S(1)} %convolution_subtract_fusion.3), custom_call_target="Cholesky" | custom-call | tf_op jit(solution)/shard_map/jit(cholesky)/cholesky | solution.py:16
  388.9 0.7 compare_reduce_fusion
  389.6 0.6 compare_reduce_fusion.1
  391.6 4.1 while.8
  391.6 0.6 fusion.81
  392.2 1.4 bitcast_dynamic-update-slice_fusion.8
  393.7 0.6 fusion.81
  394.3 1.4 bitcast_dynamic-update-slice_fusion.8
  395.7 19.7 %custom-call.20 = f32[2,128,128]{1,2,0:T(8,128)S(1)} custom-call(f32[2,128,128]{2,1,0:T(8,128)S(1)} %get-tuple-element.26), custom_call_target="InvertDiagBlocksLowerTriangular" | custom-call | tf_op jit(solution)/shard_map/triangular_solve/custom-call.0 | solution.py:17
  415.4 0.4 fusion.15
  415.8 0.6 convolution_subtract_fusion
  416.4 0.4 fusion.24
  416.9 1.9 fusion.13
  418.8 1.6 copy.18
  420.4 17.2 %all-to-all-start = ((f32[256,4,256]{2,1,0:T(4,128)}), f32[256,4,256]{2,1,0:T(4,128)S(1)}, u32[]{:S(2)}, u32[]{:S(2)}) async-start(f32[256,4,256]{2,1,0:T(4,128)} %copy.18), calls=%async_computation | async-start | bytes 2097152 | tf_op jit(solution)/shard_map/all_to_all | solution.py:34
  437.6 1.0 copy.20
  438.6 16.1 %all-to-all-done = f32[256,4,256]{2,1,0:T(4,128)S(1)} async-done(((f32[256,4,256]{2,1,0:T(4,128)}), f32[256,4,256]{2,1,0:T(4,128)S(1)}, u32[]{:S(2)}, u32[]{:S(2)}) %all-to-all-start) | async-done | bytes 1048608 | tf_op jit(solution)/shard_map/all_to_all | solution.py:34
  455.0 1.3 all_to_all.16
  (43 shorter events, 1.3 us)
Async XLA Ops:
  7.2 7.5 %copy-start = (f32[512,256]{1,0:T(8,128)S(1)}, f32[512,256]{1,0:T(8,128)}, u32[]{:S(2)}) copy-start(f32[512,256]{1,0:T(8,128)} %param.6) | copy-start | bytes 1572868
  7.2 148.4 %all-reduce.4.cloned.1.call-start = ((), (), s32[]{:S(2)}) async-start(), calls=%async_computation.1 | async-start | bytes 2097152 | tf_op jit(solution)/shard_map/psum | solution.py:28
  14.4 272.9 %all-reduce.6.cloned.1.call-start = ((), (), s32[]{:S(2)}) async-start(), calls=%async_computation.2 | async-start | bytes 2097152 | tf_op jit(solution)/shard_map/psum | solution.py:28
  15.8 163.8 %copy-start.2 = (f32[512,4,256]{2,1,0:T(4,128)S(1)}, f32[512,4,256]{2,1,0:T(4,128)}, u32[]{:S(2)}) copy-start(f32[512,4,256]{2,1,0:T(4,128)} %param.5) | copy-start | bytes 6291460
  351.1 1.5 copy-start.1
  420.4 34.3 %all-to-all-start = ((f32[256,4,256]{2,1,0:T(4,128)}), f32[256,4,256]{2,1,0:T(4,128)S(1)}, u32[]{:S(2)}, u32[]{:S(2)}) async-start(f32[256,4,256]{2,1,0:T(4,128)} %copy.18), calls=%async_computation | async-start | bytes 2097152 | tf_op jit(solution)/shard_map/all_to_all | solution.py:34
Sparse Core Ops, SparseCore 0:
  14.5 141.0 all-reduce.3
  158.1 129.1 all-reduce.5
